TPU v7x, 512 devices: a whole 4x8x8 slice. The times are simulated.
512 devices in a mesh: dp: 16 (over z, core), expert: 32 (over x, y).
Axes of the slice: x: 4, y: 8, z: 8, core: 2. Of those that a mesh axis runs over, the one named last changes fastest.
Arguments:
- residual_in: bfloat16 [16384, 2048], P(('dp', 'expert')), may hold values from -6 to 6
- attention_out: bfloat16 [16384, 2048], P(('dp', 'expert')), may hold values from -6 to 6
- out_weight: bfloat16 [2048, 2048], P(None, 'dp'), may hold values from -0.125 to 0.125
- post_gain: float32 [2048], replicated, may hold values from 0.1 to 1.9
- router_weight: bfloat16 [2048, 32], replicated, may hold values from -0.125 to 0.125
- expert_ids: int32 [16384, 6], P(('dp', 'expert')), may hold values from 0 to 31, all different within a row; in each aligned block of 32 rows (0 to 31, 32 to 63, ...) at most 12 rows name the same one
- expert_slot: int32 [32], replicated, may hold values from 0 to 31, each once
- expert_gate_up: bfloat16 [32, 2048, 1408], P('expert', 'dp'), may hold values from -0.125 to 0.125
- expert_down: bfloat16 [32, 704, 2048], P('expert', None, 'dp'), may hold values from -0.21875 to 0.21875
- shared_gate_up: bfloat16 [2048, 2, 2816], P(None, None, 'dp'), may hold values from -0.125 to 0.125
- shared_down: bfloat16 [2816, 2048], P(None, 'dp'), may hold values from -0.109375 to 0.109375
- final_gain: float32 [2048], replicated, may hold values from 0.1 to 1.9
Outputs:
- mixed: bfloat16 [16384, 2048], P(('dp', 'expert'))
Inputs may be any that keep to these rules, and one draw needn't show every extreme that they name: `expert_ids`: each row names 6 different experts. In each aligned block of 32 rows (the rows of one device) no expert is named by more than 12 rows, a bound that some block reaches. A permutation: expert e is held in slot expert_slot[e].
All inputs are finite; a program needn't handle non-finite values.
Results may differ from a plain program's by a relative error of at most 0.0069.
Values may be sent and summed in bfloat16 or wider, within the bound.
No kernel may reach another device: no remote copies, remote signals or barrier semaphores. Data moves between devices by JAX's collectives and lax.ppermute only.
A program may use at most 64 MiB of HBM per device.

v0:
```python
import jax
import jax.numpy as jnp
from jax import lax
from jax.sharding import PartitionSpec as P

EPS = 1e-06


def core_groups(axis):
    n = lax.axis_size(axis)
    return [list(range(0, n, 2)), list(range(1, n, 2))]


def with_sibling(blocks, axis):
    other = lax.ppermute(blocks, axis, [(i, i ^ 1) for i in range(lax.axis_size(axis))])
    pair = jnp.stack([blocks, other], axis=1)
    pair = jnp.where(lax.axis_index(axis) % 2 == 0, pair, jnp.flip(pair, axis=1))
    return pair.reshape(-1, *blocks.shape[1:])


def pair_gather(array, axis):
    blocks = lax.all_gather(array, axis, axis=0, axis_index_groups=core_groups(axis))
    return with_sibling(blocks, axis)


def pair_collect(array, axis):
    copies = jnp.broadcast_to(array, (lax.axis_size(axis) // 2, *array.shape))
    blocks = lax.all_to_all(copies, axis, 0, 0, tiled=True, axis_index_groups=core_groups(axis))
    return with_sibling(blocks, axis)


def in_order(blocks, dim):
    shape = list(blocks.shape[1:])
    shape[dim] *= blocks.shape[0]
    return jnp.moveaxis(blocks, 0, dim).reshape(shape)


def sent_to_all(array, axis):
    copies = jnp.broadcast_to(array, (lax.axis_size(axis), *array.shape))
    return lax.all_to_all(copies, axis, split_axis=0, concat_axis=0, tiled=True)


def collect(array, axis, dim):
    return in_order(sent_to_all(array, axis), dim)


def turned_gather(arrays, axis, dims):
    turned = [jnp.moveaxis(a, dim, 0) for a, dim in zip(arrays, dims)]
    widths = [t[0].size for t in turned]
    both = jnp.concatenate([t.reshape(-1, w) for t, w in zip(turned, widths)], axis=1)
    out = lax.all_gather(both, axis, axis=0, tiled=True)
    blocks = jnp.split(out, [sum(widths[:k]) for k in range(1, len(widths))], axis=1)
    return tuple(
        (
            jnp.moveaxis(b.reshape(-1, *t.shape[1:]), 0, dim)
            for b, t, dim in zip(blocks, turned, dims)
        )
    )


def rms_scale(values, gain):
    values = values.astype(jnp.float32)
    inverse = lax.rsqrt(jnp.mean(values * values, axis=-1, keepdims=True) + EPS)
    return values * inverse * gain


def per_device(
    residual_in,
    attention_out,
    out_weight,
    post_gain,
    router_weight,
    expert_ids,
    expert_slot,
    expert_gate_up,
    expert_down,
    shared_gate_up,
    shared_down,
    final_gain,
):
    rows = residual_in.shape[0]
    width = residual_in.shape[1]
    experts = router_weight.shape[1]
    choose = expert_ids.shape[1]
    capacity = max(2, min(rows, 2 * rows * choose // experts))
    proj_cols = jnp.dot(
        in_order(pair_collect(attention_out, "dp"), 0),
        out_weight,
        preferred_element_type=jnp.float32,
    ).astype(jnp.bfloat16)
    proj = lax.all_to_all(proj_cols, "dp", split_axis=0, concat_axis=1, tiled=True)
    resid = (residual_in.astype(jnp.float32) + proj.astype(jnp.float32)).astype(jnp.bfloat16)
    normed = rms_scale(resid, post_gain).astype(jnp.bfloat16)
    logits = jnp.dot(normed, router_weight, preferred_element_type=jnp.float32)
    expert_range = jnp.arange(experts, dtype=jnp.int32)
    ids = expert_ids + (proj_cols[0, 0] * 0).astype(expert_ids.dtype)
    picked = ids[:, :, None] == expert_range[None, None, :]
    chosen = jnp.sum(jnp.where(picked, logits[:, None, :], 0.0), axis=2)
    raised = jnp.exp(chosen)
    gates = raised / jnp.sum(raised, axis=1, keepdims=True)
    slots = jnp.sum(jnp.where(picked, expert_slot[None, None, :], 0), axis=2).reshape(-1)
    marked = (slots[:, None] == expert_range[None, :]).astype(jnp.int32)
    before = jnp.cumsum(marked, axis=0) - marked
    position = jnp.sum(before * marked, axis=1)
    target = slots * capacity + position
    placed = target[:, None] == jnp.arange(experts * capacity, dtype=jnp.int32)[None, :]
    select = jnp.any(placed.reshape(rows, choose, experts * capacity), axis=1).astype(jnp.bfloat16)
    outgoing = jnp.einsum("rs,rd->sd", select, normed, preferred_element_type=jnp.float32)
    outgoing = outgoing.astype(jnp.bfloat16).reshape(experts, capacity, width)
    hidden_units = expert_down.shape[1]
    weights_part = jnp.concatenate([expert_gate_up[0], expert_down[0].T], axis=1)
    weights_full = lax.all_gather(weights_part, "dp", axis=0, tiled=True)
    gate_up_full = weights_full[:, : 2 * hidden_units]
    down_turned_full = weights_full[:, 2 * hidden_units :]
    received = lax.all_to_all(outgoing, "expert", split_axis=0, concat_axis=0, tiled=True)
    sources, count, _ = received.shape
    flat = received.reshape(sources * count, width)
    both = jnp.dot(flat, gate_up_full, preferred_element_type=jnp.float32)
    active = (jax.nn.silu(both[:, :hidden_units]) * both[:, hidden_units:]).astype(jnp.bfloat16)
    result = lax.dot_general(
        active, down_turned_full, (((1,), (1,)), ((), ())), preferred_element_type=jnp.float32
    ).astype(jnp.bfloat16)
    result = result.reshape(sources, count, width)
    returned = lax.all_to_all(result, "expert", split_axis=0, concat_axis=0, tiled=True)
    shared_units = shared_gate_up.shape[2]
    shared_pair = shared_gate_up.reshape(width, 2 * shared_units)
    normed_shared = normed + (weights_full[0, 0] * 0 + outgoing[0, 0, 0] * 0).astype(normed.dtype)
    both = jnp.dot(
        in_order(pair_gather(normed_shared, "dp"), 0),
        shared_pair,
        preferred_element_type=jnp.float32,
    )
    shared_hidden = (jax.nn.silu(both[:, :shared_units]) * both[:, shared_units:]).astype(
        jnp.bfloat16
    )
    out_cols = jnp.dot(
        in_order(pair_gather(shared_hidden, "dp"), 1),
        shared_down,
        preferred_element_type=jnp.float32,
    )
    shared_out = lax.all_to_all(
        out_cols.astype(jnp.bfloat16), "dp", split_axis=0, concat_axis=1, tiled=True
    ).astype(jnp.float32)
    weighted = jnp.sum(placed.reshape(rows, choose, experts * capacity) * gates[:, :, None], axis=1)
    routed = jnp.dot(
        weighted,
        returned.reshape(experts * capacity, width).astype(jnp.float32),
        precision=lax.Precision.HIGHEST,
        preferred_element_type=jnp.float32,
    )
    total = resid.astype(jnp.float32) + routed + shared_out
    return rms_scale(total, final_gain).astype(jnp.bfloat16)


def solution(mesh):
    in_specs = (
        P(("dp", "expert"), None),
        P(("dp", "expert"), None),
        P(None, "dp"),
        P(),
        P(),
        P(("dp", "expert"), None),
        P(),
        P("expert", "dp", None),
        P("expert", None, "dp"),
        P(None, None, "dp"),
        P(None, "dp"),
        P(),
    )
    out_specs = P(("dp", "expert"), None)
    return jax.shard_map(
        per_device, mesh=mesh, in_specs=in_specs, out_specs=out_specs, check_vma=False
    )
```

profile of v0, /device:TPU:1, one launch (start us, length us, event | category | flops | bytes accessed | tf_op | source)
XLA Modules:
  0.0 248.7 jit_solution(5507769714941726172)
XLA Ops:
  6.5 1.2 copy.43
  7.7 1.8 pad_maximum_fusion.3
  9.6 0.1 broadcast_in_dim.26
  9.7 44.2 %all_to_all.41 = bf16[8,32,2048]{2,1,0:T(8,128)(2,1)S(1)} all-to-all(bf16[8,32,2048]{2,1,0:T(8,128)(2,1)S(1)} %broadcast_in_dim.26), channel_id=1, replica_groups={{0,64,128,192,256,320,384,448},{32,96,160,224,288,352,416,480},{1,65,12..., dimensions={0} | all-to-all | bytes 2097152 | tf_op jit(solution)/shard_map/all_to_all | solution.py:28
  53.9 5.5 %collective-permute-start = (bf16[8,32,2048]{2,1,0:T(8,128)(2,1)S(1)}, bf16[8,32,2048]{2,1,0:T(8,128)(2,1)S(1)}, u32[]{:S(2)}, u32[]{:S(2)}) collective-permute-start(bf16[8,32,2048]{2,1,0:T(8,128)(2,1)S(1)} %all_to_all.41), channel_id=1, source_target_pairs={{0,32},{32,0},{64,96},{96,64},{128,160},{160,128},{192,224},{224,1... | collective-permute-start | bytes 3145736 | tf_op jit(solution)/shard_map/ppermute | solution.py:15
  59.5 2.3 collective-permute-done
  61.8 0.2 pad_maximum_fusion.1
  62.0 0.6 reverse_select_fusion.2
  62.6 0.4 copy-done.5
  63.0 1.4 convolution_convert_fusion.1
  64.4 1.2 slice.48
  66.1 3.7 %all-to-all-start.1 = ((bf16[16,32,128]{2,1,0:T(8,128)(2,1)}), bf16[16,32,128]{2,1,0:T(8,128)(2,1)S(1)}, u32[]{:S(2)}, u32[]{:S(2)}) async-start(bf16[16,32,128]{2,1,0:T(8,128)(2,1)} %bitcast.4), calls=%async_computation.1 | async-start | bytes 262144 | tf_op jit(solution)/shard_map/all_to_all | solution.py:91
  69.8 0.0 all-gather.8.cloned.1.call-start
  69.9 0.3 select_reduce_fusion.2
  70.1 0.1 copy.39
  70.2 0.1 eq.62
  70.4 0.6 reduce-window.6
  71.0 0.2 slice_reduce_fusion
  71.2 0.1 bitcast_bitcast_fusion
  71.3 0.1 reduce_sum.67
  71.4 0.1 copy.42
  71.5 0.1 fusion.12
  71.6 8.8 %all-to-all-done.1 = bf16[16,32,128]{2,1,0:T(8,128)(2,1)S(1)} async-done(((bf16[16,32,128]{2,1,0:T(8,128)(2,1)}), bf16[16,32,128]{2,1,0:T(8,128)(2,1)S(1)}, u32[]{:S(2)}, u32[]{:S(2)}) %all-to-all-start.1) | async-done | bytes 131104 | tf_op jit(solution)/shard_map/all_to_all | solution.py:91
  80.5 0.2 fusion.13
  80.7 0.6 convolution_convert_fusion
  81.3 1.6 reshape.112
  82.9 1.2 slice.56
  84.7 8.7 %all-gather.6.cloned.1.call-done = bf16[2048,2112]{1,0:T(8,128)(2,1)} async-done(((bf16[128,2112]{1,0:T(8,128)(2,1)}), bf16[2048,2112]{1,0:T(8,128)(2,1)}) %all-gather.6.cloned.1.call-update) | async-done | bytes 8650768 | tf_op jit(solution)/shard_map/all_gather | solution.py:112
  93.4 1.2 slice.55
  95.3 0.8 broadcast_add_fusion
  96.1 9.7 %all-to-all-start.2 = ((bf16[32,12,2048]{2,1,0:T(8,128)(2,1)}), bf16[32,12,2048]{2,1,0:T(8,128)(2,1)S(1)}, u32[]{:S(2)}, u32[]{:S(2)}) async-start(bf16[32,12,2048]{2,1,0:T(8,128)(2,1)} %reshape.112), calls=%async_computation.2 | async-start | bytes 4194304 | tf_op jit(solution)/shard_map/all_to_all | solution.py:115
  105.8 0.0 all-gather.10.cloned.1.call-start
  105.8 26.9 %all-gather.8.cloned.1.call-done = bf16[256,2048]{1,0:T(8,128)(2,1)} async-done(((bf16[32,2048]{1,0:T(8,128)(2,1)}), bf16[256,2048]{1,0:T(8,128)(2,1)}) %all-gather.8.cloned.1.call-update) | async-done | bytes 1048592 | tf_op jit(solution)/shard_map/all_gather | solution.py:22
  132.8 6.4 %collective-permute-start.1 = (bf16[8,32,2048]{2,1,0:T(8,128)(2,1)}, bf16[8,32,2048]{2,1,0:T(8,128)(2,1)S(1)}, u32[]{:S(2)}, u32[]{:S(2)}) collective-permute-start(bf16[8,32,2048]{2,1,0:T(8,128)(2,1)} %bitcast.86), channel_id=1, source_target_pairs={{0,32},{32,0},{64,96},{96,64},{128,160},{160,128},{192,224},{224,1... | collective-permute-start | bytes 3145736 | tf_op jit(solution)/shard_map/ppermute | solution.py:15
  139.2 2.5 collective-permute-done.1
  141.6 1.4 pad_maximum_fusion.2
  143.1 0.6 reverse_select_fusion.1
  143.6 1.0 fusion.24
  144.6 0.8 fusion.11
  145.4 9.3 %all-to-all-done.2 = bf16[32,12,2048]{2,1,0:T(8,128)(2,1)S(1)} async-done(((bf16[32,12,2048]{2,1,0:T(8,128)(2,1)}), bf16[32,12,2048]{2,1,0:T(8,128)(2,1)S(1)}, u32[]{:S(2)}, u32[]{:S(2)}) %all-to-all-start.2) | async-done | bytes 1572896 | tf_op jit(solution)/shard_map/all_to_all | solution.py:115
  154.7 1.3 reshape.113
  156.0 5.8 %fusion = f32[384,1408]{1,0:T(8,128)S(1)} fusion(bf16[384,2048]{1,0:T(8,128)(2,1)} %reshape.113, bf16[2048,2112]{1,0:T(8,128)(2,1)} %all-gather.6.cloned.1.call-done), kind=kOutput, calls=%fused_computation | convolution fusion | flops 2214592512 | bytes 9502720 | tf_op jit(solution)/shard_map/dot_general | solution.py:118
  161.8 3.3 %fusion.4 = bf16[384,2048]{1,0:T(8,128)(2,1)S(1)} fusion(bf16[2048,2112]{1,0:T(8,128)(2,1)} %all-gather.6.cloned.1.call-done, f32[384,1408]{1,0:T(8,128)S(1)} %fusion), kind=kOutput, calls=%fused_computation.8 | convolution fusion | flops 1109704704 | bytes 7077888 | tf_op jit(solution)/shard_map/dot_general | solution.py:120
  165.2 1.5 reshape.114
  166.7 7.5 %all-to-all-start.3 = ((bf16[32,12,2048]{2,1,0:T(8,128)(2,1)}), bf16[32,12,2048]{2,1,0:T(8,128)(2,1)S(1)}, u32[]{:S(2)}, u32[]{:S(2)}) async-start(bf16[32,12,2048]{2,1,0:T(8,128)(2,1)} %reshape.114), calls=%async_computation.3 | async-start | bytes 4194304 | tf_op jit(solution)/shard_map/all_to_all | solution.py:124
  174.2 7.8 %all-gather.10.cloned.1.call-done = bf16[4096,176]{0,1:T(8,128)(2,1)} async-done(((bf16[512,176]{0,1:T(8,128)(2,1)}), bf16[4096,176]{0,1:T(8,128)(2,1)}) %all-gather.10.cloned.1.call-update) | async-done | bytes 1441808 | tf_op jit(solution)/shard_map/all_gather | solution.py:22
  182.0 1.6 copy.60
  183.6 7.3 %collective-permute-start.2 = (bf16[8,512,176]{1,2,0:T(8,128)(2,1)S(1)}, bf16[8,512,176]{1,2,0:T(8,128)(2,1)S(1)}, u32[]{:S(2)}, u32[]{:S(2)}) collective-permute-start(bf16[8,512,176]{1,2,0:T(8,128)(2,1)S(1)} %bitcast.83), channel_id=1, source_target_pairs={{0,32},{32,0},{64,96},{96,64},{128,160},{160,128},{192,224},{224,1... | collective-permute-start | bytes 4325384 | tf_op jit(solution)/shard_map/ppermute | solution.py:15
  191.0 0.2 fusion.21
  191.2 0.2 select_reduce_fusion.1
  191.4 0.6 copy.53
  192.0 0.5 copy.46
  192.5 1.1 collective-permute-done.2
  193.6 0.3 pad_maximum_fusion
  193.9 0.6 reverse_select_fusion
  194.5 0.5 copy-done.4
  195.0 1.6 convolution_convert_fusion.2
  196.6 26.5 %all-to-all-done.3 = bf16[32,12,2048]{2,1,0:T(8,128)(2,1)S(1)} async-done(((bf16[32,12,2048]{2,1,0:T(8,128)(2,1)}), bf16[32,12,2048]{2,1,0:T(8,128)(2,1)S(1)}, u32[]{:S(2)}, u32[]{:S(2)}) %all-to-all-start.3) | async-done | bytes 1572896 | tf_op jit(solution)/shard_map/all_to_all | solution.py:124
  223.1 6.7 %all-to-all-start.4 = ((bf16[16,32,128]{2,1,0:T(8,128)(2,1)}), bf16[16,32,128]{2,1,0:T(8,128)(2,1)}, u32[]{:S(2)}, u32[]{:S(2)}) async-start(bf16[16,32,128]{2,1,0:T(8,128)(2,1)} %bitcast.90), calls=%async_computation.4 | async-start | bytes 262144 | tf_op jit(solution)/shard_map/all_to_all | solution.py:141
  229.8 0.7 select_reduce_fusion
  230.5 1.3 reshape.115
  231.8 7.2 %all-to-all-done.4 = bf16[16,32,128]{2,1,0:T(8,128)(2,1)} async-done(((bf16[16,32,128]{2,1,0:T(8,128)(2,1)}), bf16[16,32,128]{2,1,0:T(8,128)(2,1)}, u32[]{:S(2)}, u32[]{:S(2)}) %all-to-all-start.4) | async-done | bytes 131104 | tf_op jit(solution)/shard_map/all_to_all | solution.py:141
  239.0 2.4 multiply_reduce_fusion
  241.4 0.8 multiply_convert_fusion
  (43 shorter events, 0.3 us)
Async XLA Ops:
  6.5 137.1 %copy-start = (bf16[2048,2,176]{0,2,1:T(8,128)(2,1)S(1)}, bf16[2048,2,176]{0,2,1:T(8,128)(2,1)}, u32[]{:S(2)}) copy-start(bf16[2048,2,176]{0,2,1:T(8,128)(2,1)} %param.21) | copy-start | bytes 4325380
  6.5 3.0 %copy-start.6 = (bf16[32,2048]{1,0:T(8,128)(2,1)S(1)}, bf16[32,2048]{1,0:T(8,128)(2,1)}, u32[]{:S(2)}) copy-start(bf16[32,2048]{1,0:T(8,128)(2,1)} %param.13) | copy-start | bytes 393220
  6.5 86.9 %all-gather.6.cloned.1.call-start = ((), (), s32[]{:S(2)}) async-start(), calls=%async_computation.5 | async-start | bytes 9469952 | tf_op jit(solution)/shard_map/all_gather | solution.py:112
  53.9 7.8 %collective-permute-start = (bf16[8,32,2048]{2,1,0:T(8,128)(2,1)S(1)}, bf16[8,32,2048]{2,1,0:T(8,128)(2,1)S(1)}, u32[]{:S(2)}, u32[]{:S(2)}) collective-permute-start(bf16[8,32,2048]{2,1,0:T(8,128)(2,1)S(1)} %all_to_all.41), channel_id=1, source_target_pairs={{0,32},{32,0},{64,96},{96,64},{128,160},{160,128},{192,224},{224,1... | collective-permute-start | bytes 3145736 | tf_op jit(solution)/shard_map/ppermute | solution.py:15
  62.0 1.0 copy-start.5
  62.5 7.3 %copy-start.10 = (s32[32,6]{0,1:T(8,128)S(1)}, s32[32,6]{0,1:T(8,128)}, u32[]{:S(2)}) copy-start(s32[32,6]{0,1:T(8,128)} %param.17) | copy-start | bytes 2308
  62.6 7.3 %copy-start.13 = (s32[32]{0:T(128)S(1)}, s32[32]{0:T(128)}, u32[]{:S(2)}) copy-start(s32[32]{0:T(128)} %param.18) | copy-start | bytes 388
  62.6 17.9 %copy-start.7 = (bf16[32,2048]{1,0:T(8,128)(2,1)S(1)}, bf16[32,2048]{1,0:T(8,128)(2,1)}, u32[]{:S(2)}) copy-start(bf16[32,2048]{1,0:T(8,128)(2,1)} %param.12) | copy-start | bytes 393220
  62.6 18.1 %copy-start.8 = (f32[2048]{0:T(1024)S(1)}, f32[2048]{0:T(1024)}, u32[]{:S(2)}) copy-start(f32[2048]{0:T(1024)} %param.15) | copy-start | bytes 24580
  66.1 14.4 %all-to-all-start.1 = ((bf16[16,32,128]{2,1,0:T(8,128)(2,1)}), bf16[16,32,128]{2,1,0:T(8,128)(2,1)S(1)}, u32[]{:S(2)}, u32[]{:S(2)}) async-start(bf16[16,32,128]{2,1,0:T(8,128)(2,1)} %bitcast.4), calls=%async_computation.1 | async-start | bytes 262144 | tf_op jit(solution)/shard_map/all_to_all | solution.py:91
  69.8 63.0 %all-gather.8.cloned.1.call-start = ((), (), s32[]{:S(2)}) async-start(), calls=%async_computation.6 | async-start | bytes 1179648 | tf_op jit(solution)/shard_map/all_gather | solution.py:22
  80.6 14.7 %copy-start.2 = (bf16[32,2048]{1,0:T(8,128)(2,1)}, bf16[32,2048]{1,0:T(8,128)(2,1)S(1)}, u32[]{:S(2)}) copy-start(bf16[32,2048]{1,0:T(8,128)(2,1)S(1)} %get-tuple-element.6) | copy-start | bytes 393220
  80.6 14.6 %copy-start.11 = (f32[32]{0:T(128)}, f32[32]{0:T(128)S(1)}, u32[]{:S(2)}) copy-start(f32[32]{0:T(128)S(1)} %add_rsqrt_fusion.1) | copy-start | bytes 388
  96.1 58.6 %all-to-all-start.2 = ((bf16[32,12,2048]{2,1,0:T(8,128)(2,1)}), bf16[32,12,2048]{2,1,0:T(8,128)(2,1)S(1)}, u32[]{:S(2)}, u32[]{:S(2)}) async-start(bf16[32,12,2048]{2,1,0:T(8,128)(2,1)} %reshape.112), calls=%async_computation.2 | async-start | bytes 4194304 | tf_op jit(solution)/shard_map/all_to_all | solution.py:115
  105.8 76.3 %all-gather.10.cloned.1.call-start = ((), (), s32[]{:S(2)}) async-start(), calls=%async_computation.7 | async-start | bytes 1622016 | tf_op jit(solution)/shard_map/all_gather | solution.py:22
  132.8 8.9 %collective-permute-start.1 = (bf16[8,32,2048]{2,1,0:T(8,128)(2,1)}, bf16[8,32,2048]{2,1,0:T(8,128)(2,1)S(1)}, u32[]{:S(2)}, u32[]{:S(2)}) collective-permute-start(bf16[8,32,2048]{2,1,0:T(8,128)(2,1)} %bitcast.86), channel_id=1, source_target_pairs={{0,32},{32,0},{64,96},{96,64},{128,160},{160,128},{192,224},{224,1... | collective-permute-start | bytes 3145736 | tf_op jit(solution)/shard_map/ppermute | solution.py:15
  166.7 56.4 %all-to-all-start.3 = ((bf16[32,12,2048]{2,1,0:T(8,128)(2,1)}), bf16[32,12,2048]{2,1,0:T(8,128)(2,1)S(1)}, u32[]{:S(2)}, u32[]{:S(2)}) async-start(bf16[32,12,2048]{2,1,0:T(8,128)(2,1)} %reshape.114), calls=%async_computation.3 | async-start | bytes 4194304 | tf_op jit(solution)/shard_map/all_to_all | solution.py:124
  182.0 8.9 %copy-start.3 = (bf16[32,2048]{1,0:T(8,128)(2,1)S(1)}, bf16[32,2048]{1,0:T(8,128)(2,1)}, u32[]{:S(2)}) copy-start(bf16[32,2048]{1,0:T(8,128)(2,1)} %copy-done.2) | copy-start | bytes 393220
  182.0 8.9 %copy-start.12 = (f32[32]{0:T(128)S(1)}, f32[32]{0:T(128)}, u32[]{:S(2)}) copy-start(f32[32]{0:T(128)} %copy-done.11) | copy-start | bytes 388
  182.0 8.9 %copy-start.14 = (bf16[2048,32]{0,1:T(8,128)(2,1)S(1)}, bf16[2048,32]{0,1:T(8,128)(2,1)}, u32[]{:S(2)}) copy-start(bf16[2048,32]{0,1:T(8,128)(2,1)} %param.16) | copy-start | bytes 393220
  182.0 9.4 %copy-start.1 = (bf16[4096,176]{0,1:T(8,128)(2,1)S(1)}, bf16[4096,176]{0,1:T(8,128)(2,1)}, u32[]{:S(2)}) copy-start(bf16[4096,176]{0,1:T(8,128)(2,1)} %all-gather.10.cloned.1.call-done) | copy-start | bytes 4325380
  183.6 9.9 %collective-permute-start.2 = (bf16[8,512,176]{1,2,0:T(8,128)(2,1)S(1)}, bf16[8,512,176]{1,2,0:T(8,128)(2,1)S(1)}, u32[]{:S(2)}, u32[]{:S(2)}) collective-permute-start(bf16[8,512,176]{1,2,0:T(8,128)(2,1)S(1)} %bitcast.83), channel_id=1, source_target_pairs={{0,32},{32,0},{64,96},{96,64},{128,160},{160,128},{192,224},{224,1... | collective-permute-start | bytes 4325384 | tf_op jit(solution)/shard_map/ppermute | solution.py:15
  193.9 1.1 copy-start.4
  223.1 16.0 %all-to-all-start.4 = ((bf16[16,32,128]{2,1,0:T(8,128)(2,1)}), bf16[16,32,128]{2,1,0:T(8,128)(2,1)}, u32[]{:S(2)}, u32[]{:S(2)}) async-start(bf16[16,32,128]{2,1,0:T(8,128)(2,1)} %bitcast.90), calls=%async_computation.4 | async-start | bytes 262144 | tf_op jit(solution)/shard_map/all_to_all | solution.py:141
  230.5 10.9 %copy-start.9 = (f32[2048]{0:T(1024)S(1)}, f32[2048]{0:T(1024)}, u32[]{:S(2)}) copy-start(f32[2048]{0:T(1024)} %param.23) | copy-start | bytes 24580
Sparse Core Ops, SparseCore 0:
  9.7 83.6 all-gather.5
  96.2 36.5 all-gather.7
  145.5 36.4 all-gather.9
where the time goes:
time: 250 us; the launch traced here: 249 us
  waiting for transfers between devices  101 us (40%)
  starting transfers between devices  46.9 us (19%)
  blocking collectives  44.2 us (18%)
  matrix products  16.3 us (7%)
  between operations  15.4 us (6%)
  local copies, waits for them, and re-layouts  14.8 us (6%)
  other arithmetic  9.99 us (4%)
    all_to_all x1, blocking collectives, pair_collect(): lax.all_to_all(copies, axis, 0, 0, tiled=True, axis_index_groups=core_gro...  44.2 us
    all_gather x2, waiting for transfers between devices, pair_gather(): lax.all_gather(array, axis, axis=0, axis_index_groups=core_groups(axis))  34.7 us
    all_to_all x1, waiting for transfers between devices, per_device(): lax.all_to_all(result, 'expert', split_axis=0, concat_axis=0, tiled=True)  26.5 us
    ppermute x3, starting transfers between devices, with_sibling(): lax.ppermute(blocks, axis, [(i, i ^ 1) for i in range(lax.axis_size(axis))])  19.2 us
    all_to_all x1, starting transfers between devices, per_device(): lax.all_to_all(outgoing, 'expert', split_axis=0, concat_axis=0, tiled=True)  9.68 us
    all_to_all x1, waiting for transfers between devices, per_device(): lax.all_to_all(outgoing, 'expert', split_axis=0, concat_axis=0, tiled=True)  9.27 us
    all_to_all x1, waiting for transfers between devices, per_device(): lax.all_to_all(proj_cols, 'dp', split_axis=0, concat_axis=1, tiled=True)  8.85 us
    all_gather x1, waiting for transfers between devices, per_device(): weights_full = lax.all_gather(weights_part, 'dp', axis=0, tiled=True)  8.74 us
  transfers between devices with their start and end apart: 10, of which 10 were waited for; matrix products, arithmetic and copies ran while one was open for 13% of the time, Pallas kernels for 0%

commit v1 on v0

--- a/solution.py
+++ b/solution.py
@@ -109,7 +109,18 @@
     outgoing = outgoing.astype(jnp.bfloat16).reshape(experts, capacity, width)
     hidden_units = expert_down.shape[1]
     weights_part = jnp.concatenate([expert_gate_up[0], expert_down[0].T], axis=1)
-    weights_full = lax.all_gather(weights_part, "dp", axis=0, tiled=True)
+    ways = lax.axis_size("dp")
+    up = [(d, (d + 1) % ways) for d in range(ways)]
+    down = [(d, (d - 1) % ways) for d in range(ways)]
+    earlier, later = ([weights_part], [weights_part])
+    for __2 in range(ways // 2):
+        earlier.append(lax.ppermute(earlier[-1], "dp", up))
+    for __2 in range((ways - 1) // 2):
+        later.append(lax.ppermute(later[-1], "dp", down))
+    line = jnp.concatenate([*earlier[::-1], *later[1:]], axis=0)
+    weights_full = jnp.roll(
+        line, (lax.axis_index("dp") - ways // 2) * weights_part.shape[0], axis=0
+    )
     gate_up_full = weights_full[:, : 2 * hidden_units]
     down_turned_full = weights_full[:, 2 * hidden_units :]
     received = lax.all_to_all(outgoing, "expert", split_axis=0, concat_axis=0, tiled=True)

time: 250 us -> 371 us (1.48)
  waiting for transfers between devices: 101 us -> 166 us
  local copies, waits for them, and re-layouts: 14.8 us -> 71.8 us
  blocking collectives: 44.2 us -> 0 us
  starting transfers between devices: 46.9 us -> 82.8 us
  other arithmetic: 9.99 us -> 14 us
    all_to_all x1 -> x0, blocking collectives: 44.2 us -> none  [pair_collect(): lax.all_to_all(copies, axis, 0, 0, tiled=True, axis_index_groups=core_gro...]
    all_to_all x1, waiting for transfers between devices: 9.27 us -> 44.8 us  [per_device(): lax.all_to_all(outgoing, 'expert', split_axis=0, concat_axis=0, tiled=True)]
    ppermute x0 -> x15, waiting for transfers between devices: none -> 33.9 us  [the longest x8 32.1 us: per_device(): earlier.append(lax.ppermute(earlier[-1], 'dp', up))]
    ppermute x0 -> x15, local copies, waits for them, and re-layouts: none -> 30.6 us  [the longest x8 15.9 us: per_device(): earlier.append(lax.ppermute(earlier[-1], 'dp', up))]
    ppermute x0 -> x15, starting transfers between devices: none -> 25.9 us  [the longest x7 13.7 us: per_device(): later.append(lax.ppermute(later[-1], 'dp', down))]
    unnamed x32 -> x91, local copies, waits for them, and re-layouts: 2.76 us -> 27.1 us
    all_to_all x1, waiting for transfers between devices: 26.5 us -> 38.1 us  [per_device(): lax.all_to_all(result, 'expert', split_axis=0, concat_axis=0, tiled=True)]
    all_to_all x0 -> x1, starting transfers between devices: none -> 10.9 us  [pair_collect(): lax.all_to_all(copies, axis, 0, 0, tiled=True, axis_index_groups=core_gro...]
  transfers between devices with their start and end apart: 10 -> 25, of which waited for: 10 -> 11; matrix products, arithmetic and copies ran while one was open for 13% -> 19% of each run, Pallas kernels for 0% -> 0%
where the time goes in v1:
time: 371 us; the launch traced here: 369 us
  waiting for transfers between devices  166 us (45%)
  starting transfers between devices  82.8 us (22%)
  local copies, waits for them, and re-layouts  71.8 us (19%)
  matrix products  18.3 us (5%)
  between operations  16.2 us (4%)
  other arithmetic  14 us (4%)
    all_to_all x1, waiting for transfers between devices, per_device(): lax.all_to_all(outgoing, 'expert', split_axis=0, concat_axis=0, tiled=True)  44.8 us
    all_to_all x1, waiting for transfers between devices, per_device(): lax.all_to_all(result, 'expert', split_axis=0, concat_axis=0, tiled=True)  38.1 us
    all_gather x2, waiting for transfers between devices, pair_gather(): lax.all_gather(array, axis, axis=0, axis_index_groups=core_groups(axis))  35.6 us
    ppermute x8, waiting for transfers between devices, per_device(): earlier.append(lax.ppermute(earlier[-1], 'dp', up))  32.1 us
    unnamed x91, local copies, waits for them, and re-layouts  27.1 us
    ppermute x8, local copies, waits for them, and re-layouts, per_device(): earlier.append(lax.ppermute(earlier[-1], 'dp', up))  15.9 us
    ppermute x7, local copies, waits for them, and re-layouts, per_device(): later.append(lax.ppermute(later[-1], 'dp', down))  14.7 us
    ppermute x3, starting transfers between devices, with_sibling(): lax.ppermute(blocks, axis, [(i, i ^ 1) for i in range(lax.axis_size(axis))])  14.6 us
  transfers between devices with their start and end apart: 25, of which 11 were waited for; matrix products, arithmetic and copies ran while one was open for 19% of the time, Pallas kernels for 0%

profile of v1, /device:TPU:1, one launch (start us, length us, event | category | flops | bytes accessed | tf_op | source)
XLA Modules:
  0.0 369.0 jit_solution(14875731956277678673)
XLA Ops:
  6.5 2.1 broadcast_in_dim.26
  8.6 10.9 %all-to-all-start = ((bf16[8,32,2048]{2,1,0:T(8,128)(2,1)}), bf16[8,32,2048]{2,1,0:T(8,128)(2,1)S(1)}, u32[]{:S(2)}, u32[]{:S(2)}) async-start(bf16[8,32,2048]{2,1,0:T(8,128)(2,1)} %broadcast_in_dim.26), calls=%async_computation | async-start | bytes 2097152 | tf_op jit(solution)/shard_map/all_to_all | solution.py:28
  22.7 2.6 collective-permute-start.1
  25.3 23.3 %collective-permute-done.1 = bf16[128,2112]{0,1:T(8,128)(2,1)S(1)} collective-permute-done((bf16[128,2112]{0,1:T(8,128)(2,1)}, bf16[128,2112]{0,1:T(8,128)(2,1)S(1)}, u32[]{:S(2)}, u32[]{:S(2)}) %collective-permute-start.1) | collective-permute-done | bytes 540704 | tf_op jit(solution)/shard_map/ppermute | solution.py:117
  48.6 2.4 collective-permute-start.2
  51.0 1.3 collective-permute-start.10
  52.3 5.0 %collective-permute-done.2 = bf16[128,2112]{0,1:T(8,128)(2,1)S(1)} collective-permute-done((bf16[128,2112]{0,1:T(8,128)(2,1)S(1)}, bf16[128,2112]{0,1:T(8,128)(2,1)S(1)}, u32[]{:S(2)}, u32[]{:S(2)}) %collective-permute-start.2) | collective-permute-done | bytes 540704 | tf_op jit(solution)/shard_map/ppermute | solution.py:117
  57.3 2.5 collective-permute-start.3
  60.1 2.2 collective-permute-start.11
  62.3 3.8 %collective-permute-done.3 = bf16[128,2112]{0,1:T(8,128)(2,1)} collective-permute-done((bf16[128,2112]{0,1:T(8,128)(2,1)S(1)}, bf16[128,2112]{0,1:T(8,128)(2,1)}, u32[]{:S(2)}, u32[]{:S(2)}) %collective-permute-start.3) | collective-permute-done | bytes 540704 | tf_op jit(solution)/shard_map/ppermute | solution.py:117
  66.1 2.6 collective-permute-start.4
  69.3 3.1 collective-permute-start.12
  72.4 4.8 %collective-permute-start = (bf16[8,32,2048]{2,1,0:T(8,128)(2,1)S(1)}, bf16[8,32,2048]{2,1,0:T(8,128)(2,1)}, u32[]{:S(2)}, u32[]{:S(2)}) collective-permute-start(bf16[8,32,2048]{2,1,0:T(8,128)(2,1)S(1)} %all-to-all-done), channel_id=1, source_target_pairs={{0,32},{32,0},{64,96},{96,64},{128,160},{160,128},{192,224},{224,1... | collective-permute-start | bytes 3145736 | tf_op jit(solution)/shard_map/ppermute | solution.py:15
  78.7 4.0 %collective-permute-start.13 = (bf16[128,2112]{0,1:T(8,128)(2,1)}, bf16[128,2112]{0,1:T(8,128)(2,1)}, u32[]{:S(2)}, u32[]{:S(2)}) collective-permute-start(bf16[128,2112]{0,1:T(8,128)(2,1)} %collective-permute-done.12), channel_id=1, source_target_pairs={{0,480},{32,0},{64,32},{96,64},{128,96},{160,128},{192,160},{224,1... | collective-permute-start | bytes 1622024 | tf_op jit(solution)/shard_map/ppermute | solution.py:119
  83.8 2.1 copy.86
  85.9 2.1 copy.84
  88.0 2.1 copy.87
  90.1 2.1 copy.83
  92.2 2.1 copy.88
  94.3 2.1 copy.82
  96.4 2.1 copy.89
  98.5 2.1 copy.81
  100.7 2.1 copy.90
  102.8 3.0 collective-permute-start.14
  105.7 1.4 pad_maximum_fusion.1
  107.7 2.4 convolution_convert_fusion.1
  110.1 1.3 slice.48
  113.8 7.8 %all-to-all-start.1 = ((bf16[16,32,128]{2,1,0:T(8,128)(2,1)}), bf16[16,32,128]{2,1,0:T(8,128)(2,1)S(1)}, u32[]{:S(2)}, u32[]{:S(2)}) async-start(bf16[16,32,128]{2,1,0:T(8,128)(2,1)} %bitcast.4), calls=%async_computation.1 | async-start | bytes 262144 | tf_op jit(solution)/shard_map/all_to_all | solution.py:91
  121.9 1.6 collective-permute-start.8
  123.5 6.2 %all-to-all-done.1 = bf16[16,32,128]{2,1,0:T(8,128)(2,1)S(1)} async-done(((bf16[16,32,128]{2,1,0:T(8,128)(2,1)}), bf16[16,32,128]{2,1,0:T(8,128)(2,1)S(1)}, u32[]{:S(2)}, u32[]{:S(2)}) %all-to-all-start.1) | async-done | bytes 131104 | tf_op jit(solution)/shard_map/all_to_all | solution.py:91
  131.3 1.5 reshape.112
  132.8 1.4 slice.53
  134.8 2.1 copy.80
  136.9 2.1 copy.91
  138.9 2.2 copy.79
  141.1 2.1 copy.92
  143.2 2.2 copy.78
  145.5 1.2 constant_dynamic-update-slice_fusion.31
  146.7 1.8 constant_dynamic-update-slice_fusion.30
  148.5 1.1 constant_dynamic-update-slice_fusion.29
  150.7 1.1 constant_dynamic-update-slice_fusion.27
  164.1 6.1 %copy-done.26 = bf16[4096,2112]{1,0:T(8,128)(2,1)} copy-done((bf16[4096,2112]{1,0:T(8,128)(2,1)}, bf16[4096,2112]{1,0:T(8,128)(2,1)S(1)}, u32[]{:S(2)}) %copy-start.26) | copy-done | bytes 17301528
  171.4 1.7 broadcast_add_fusion
  173.1 35.6 %all-gather.5.cloned.1.call-done = bf16[256,2048]{1,0:T(8,128)(2,1)} async-done(((bf16[32,2048]{1,0:T(8,128)(2,1)}), bf16[256,2048]{1,0:T(8,128)(2,1)}) %all-gather.5.cloned.1.call-update) | async-done | bytes 1048592 | tf_op jit(solution)/shard_map/all_gather | solution.py:22
  208.7 7.1 %collective-permute-start.16 = (bf16[8,32,2048]{2,1,0:T(8,128)(2,1)}, bf16[8,32,2048]{2,1,0:T(8,128)(2,1)}, u32[]{:S(2)}, u32[]{:S(2)}) collective-permute-start(bf16[8,32,2048]{2,1,0:T(8,128)(2,1)} %bitcast.91), channel_id=1, source_target_pairs={{0,32},{32,0},{64,96},{96,64},{128,160},{160,128},{192,224},{224,1... | collective-permute-start | bytes 3145736 | tf_op jit(solution)/shard_map/ppermute | solution.py:15
  215.8 9.3 %all-to-all-start.2 = ((bf16[32,12,2048]{2,1,0:T(8,128)(2,1)}), bf16[32,12,2048]{2,1,0:T(8,128)(2,1)S(1)}, u32[]{:S(2)}, u32[]{:S(2)}) async-start(bf16[32,12,2048]{2,1,0:T(8,128)(2,1)} %reshape.112), calls=%async_computation.2 | async-start | bytes 4194304 | tf_op jit(solution)/shard_map/all_to_all | solution.py:126
  225.3 1.7 pad_maximum_fusion.2
  229.5 44.8 %all-to-all-done.2 = bf16[32,12,2048]{2,1,0:T(8,128)(2,1)S(1)} async-done(((bf16[32,12,2048]{2,1,0:T(8,128)(2,1)}), bf16[32,12,2048]{2,1,0:T(8,128)(2,1)S(1)}, u32[]{:S(2)}, u32[]{:S(2)}) %all-to-all-start.2) | async-done | bytes 1572896 | tf_op jit(solution)/shard_map/all_to_all | solution.py:126
  274.3 1.3 reshape.113
  275.6 5.7 %fusion = f32[384,1408]{1,0:T(8,128)S(1)} fusion(bf16[384,2048]{1,0:T(8,128)(2,1)} %reshape.113, bf16[4096,2112]{1,0:T(8,128)(2,1)} %copy-done.26, s32[]{:T(128)S(6)} %select_n.57), kind=kOutput, calls=%fused_computation | convolution fusion | flops 2214592512 | bytes 9502724 | tf_op jit(solution)/shard_map/dot_general | solution.py:129
  281.3 3.4 fusion.4
  284.7 1.6 reshape.114
  286.3 7.6 %all-to-all-start.3 = ((bf16[32,12,2048]{2,1,0:T(8,128)(2,1)}), bf16[32,12,2048]{2,1,0:T(8,128)(2,1)S(1)}, u32[]{:S(2)}, u32[]{:S(2)}) async-start(bf16[32,12,2048]{2,1,0:T(8,128)(2,1)} %reshape.114), calls=%async_computation.3 | async-start | bytes 4194304 | tf_op jit(solution)/shard_map/all_to_all | solution.py:135
  293.9 1.5 copy.124
  295.5 2.6 collective-permute-start.17
  298.1 1.2 fusion.22
  299.5 2.0 copy.117
  302.8 1.6 convolution_convert_fusion.2
  304.4 38.1 %all-to-all-done.3 = bf16[32,12,2048]{2,1,0:T(8,128)(2,1)S(1)} async-done(((bf16[32,12,2048]{2,1,0:T(8,128)(2,1)}), bf16[32,12,2048]{2,1,0:T(8,128)(2,1)S(1)}, u32[]{:S(2)}, u32[]{:S(2)}) %all-to-all-start.3) | async-done | bytes 1572896 | tf_op jit(solution)/shard_map/all_to_all | solution.py:135
  342.6 6.5 %all-to-all-start.4 = ((bf16[16,32,128]{2,1,0:T(8,128)(2,1)}), bf16[16,32,128]{2,1,0:T(8,128)(2,1)}, u32[]{:S(2)}, u32[]{:S(2)}) async-start(bf16[16,32,128]{2,1,0:T(8,128)(2,1)} %bitcast.93), calls=%async_computation.4 | async-start | bytes 262144 | tf_op jit(solution)/shard_map/all_to_all | solution.py:152
  349.8 1.4 reshape.115
  351.1 7.2 %all-to-all-done.4 = bf16[16,32,128]{2,1,0:T(8,128)(2,1)} async-done(((bf16[16,32,128]{2,1,0:T(8,128)(2,1)}), bf16[16,32,128]{2,1,0:T(8,128)(2,1)}, u32[]{:S(2)}, u32[]{:S(2)}) %all-to-all-start.4) | async-done | bytes 131104 | tf_op jit(solution)/shard_map/all_to_all | solution.py:152
  358.3 2.4 multiply_reduce_fusion
  360.7 1.5 multiply_convert_fusion
  (149 shorter events, 28.9 us)
Async XLA Ops:
  6.5 221.1 %copy-start = (bf16[2048,2,176]{0,2,1:T(8,128)(2,1)S(1)}, bf16[2048,2,176]{0,2,1:T(8,128)(2,1)}, u32[]{:S(2)}) copy-start(bf16[2048,2,176]{0,2,1:T(8,128)(2,1)} %param.21) | copy-start | bytes 4325380
  6.5 105.6 %copy-start.27 = (s32[32,6]{0,1:T(8,128)S(1)}, s32[32,6]{0,1:T(8,128)}, u32[]{:S(2)}) copy-start(s32[32,6]{0,1:T(8,128)} %param.17) | copy-start | bytes 2308
  6.5 105.6 %copy-start.29 = (s32[32]{0:T(128)S(1)}, s32[32]{0:T(128)}, u32[]{:S(2)}) copy-start(s32[32]{0:T(128)} %param.18) | copy-start | bytes 388
  6.5 124.1 %copy-start.25 = (f32[2048]{0:T(1024)S(1)}, f32[2048]{0:T(1024)}, u32[]{:S(2)}) copy-start(f32[2048]{0:T(1024)} %param.15) | copy-start | bytes 24580
  8.6 63.8 %all-to-all-start = ((bf16[8,32,2048]{2,1,0:T(8,128)(2,1)}), bf16[8,32,2048]{2,1,0:T(8,128)(2,1)S(1)}, u32[]{:S(2)}, u32[]{:S(2)}) async-start(bf16[8,32,2048]{2,1,0:T(8,128)(2,1)} %broadcast_in_dim.26), calls=%async_computation | async-start | bytes 2097152 | tf_op jit(solution)/shard_map/all_to_all | solution.py:28
  20.6 109.4 %copy-start.17 = (bf16[1,704,128]{1,2,0:T(8,128)(2,1)}, bf16[1,704,128]{1,2,0:T(8,128)(2,1)S(1)}, u32[]{:S(2)}) copy-start(bf16[1,704,128]{1,2,0:T(8,128)(2,1)S(1)} %copy.75) | copy-start | bytes 540676
  22.7 25.9 %collective-permute-start.1 = (bf16[128,2112]{0,1:T(8,128)(2,1)}, bf16[128,2112]{0,1:T(8,128)(2,1)S(1)}, u32[]{:S(2)}, u32[]{:S(2)}) collective-permute-start(bf16[128,2112]{0,1:T(8,128)(2,1)} %copy.76), channel_id=1, source_target_pairs={{0,32},{32,64},{64,96},{96,128},{128,160},{160,192},{192,224},{224... | collective-permute-start | bytes 1622024 | tf_op jit(solution)/shard_map/ppermute | solution.py:117
  25.3 25.7 %collective-permute-start.9 = (bf16[128,2112]{0,1:T(8,128)(2,1)}, bf16[128,2112]{0,1:T(8,128)(2,1)S(1)}, u32[]{:S(2)}, u32[]{:S(2)}) collective-permute-start(bf16[128,2112]{0,1:T(8,128)(2,1)} %copy.76), channel_id=1, source_target_pairs={{0,480},{32,0},{64,32},{96,64},{128,96},{160,128},{192,160},{224,1... | collective-permute-start | bytes 1622024 | tf_op jit(solution)/shard_map/ppermute | solution.py:119
  48.6 8.7 %collective-permute-start.2 = (bf16[128,2112]{0,1:T(8,128)(2,1)S(1)}, bf16[128,2112]{0,1:T(8,128)(2,1)S(1)}, u32[]{:S(2)}, u32[]{:S(2)}) collective-permute-start(bf16[128,2112]{0,1:T(8,128)(2,1)S(1)} %collective-permute-done.1), channel_id=1, source_target_pairs={{0,32},{32,64},{64,96},{96,128},{128,160},{160,192},{192,224},{224... | collective-permute-start | bytes 1622024 | tf_op jit(solution)/shard_map/ppermute | solution.py:117
  51.0 18.3 %copy-start.21 = (bf16[128,2112]{0,1:T(8,128)(2,1)}, bf16[128,2112]{0,1:T(8,128)(2,1)S(1)}, u32[]{:S(2)}) copy-start(bf16[128,2112]{0,1:T(8,128)(2,1)S(1)} %collective-permute-done.9) | copy-start | bytes 1622020
  51.0 9.1 %collective-permute-start.10 = (bf16[128,2112]{0,1:T(8,128)(2,1)S(1)}, bf16[128,2112]{0,1:T(8,128)(2,1)S(1)}, u32[]{:S(2)}, u32[]{:S(2)}) collective-permute-start(bf16[128,2112]{0,1:T(8,128)(2,1)S(1)} %collective-permute-done.9), channel_id=1, source_target_pairs={{0,480},{32,0},{64,32},{96,64},{128,96},{160,128},{192,160},{224,1... | collective-permute-start | bytes 1622024 | tf_op jit(solution)/shard_map/ppermute | solution.py:119
  57.3 12.0 %copy-start.22 = (bf16[128,2112]{0,1:T(8,128)(2,1)}, bf16[128,2112]{0,1:T(8,128)(2,1)S(1)}, u32[]{:S(2)}) copy-start(bf16[128,2112]{0,1:T(8,128)(2,1)S(1)} %collective-permute-done.2) | copy-start | bytes 1622020
  57.3 8.8 %collective-permute-start.3 = (bf16[128,2112]{0,1:T(8,128)(2,1)S(1)}, bf16[128,2112]{0,1:T(8,128)(2,1)}, u32[]{:S(2)}, u32[]{:S(2)}) collective-permute-start(bf16[128,2112]{0,1:T(8,128)(2,1)S(1)} %collective-permute-done.2), channel_id=1, source_target_pairs={{0,32},{32,64},{64,96},{96,128},{128,160},{160,192},{192,224},{224... | collective-permute-start | bytes 1622024 | tf_op jit(solution)/shard_map/ppermute | solution.py:117
  60.1 9.2 %copy-start.23 = (bf16[128,2112]{0,1:T(8,128)(2,1)}, bf16[128,2112]{0,1:T(8,128)(2,1)S(1)}, u32[]{:S(2)}) copy-start(bf16[128,2112]{0,1:T(8,128)(2,1)S(1)} %collective-permute-done.10) | copy-start | bytes 1622020
  60.1 9.2 %collective-permute-start.11 = (bf16[128,2112]{0,1:T(8,128)(2,1)S(1)}, bf16[128,2112]{0,1:T(8,128)(2,1)}, u32[]{:S(2)}, u32[]{:S(2)}) collective-permute-start(bf16[128,2112]{0,1:T(8,128)(2,1)S(1)} %collective-permute-done.10), channel_id=1, source_target_pairs={{0,480},{32,0},{64,32},{96,64},{128,96},{160,128},{192,160},{224,1... | collective-permute-start | bytes 1622024 | tf_op jit(solution)/shard_map/ppermute | solution.py:119
  66.1 11.2 %collective-permute-start.4 = (bf16[128,2112]{0,1:T(8,128)(2,1)}, bf16[128,2112]{0,1:T(8,128)(2,1)}, u32[]{:S(2)}, u32[]{:S(2)}) collective-permute-start(bf16[128,2112]{0,1:T(8,128)(2,1)} %collective-permute-done.3), channel_id=1, source_target_pairs={{0,32},{32,64},{64,96},{96,128},{128,160},{160,192},{192,224},{224... | collective-permute-start | bytes 1622024 | tf_op jit(solution)/shard_map/ppermute | solution.py:117
  69.3 9.4 %collective-permute-start.12 = (bf16[128,2112]{0,1:T(8,128)(2,1)}, bf16[128,2112]{0,1:T(8,128)(2,1)}, u32[]{:S(2)}, u32[]{:S(2)}) collective-permute-start(bf16[128,2112]{0,1:T(8,128)(2,1)} %collective-permute-done.11), channel_id=1, source_target_pairs={{0,480},{32,0},{64,32},{96,64},{128,96},{160,128},{192,160},{224,1... | collective-permute-start | bytes 1622024 | tf_op jit(solution)/shard_map/ppermute | solution.py:119
  72.4 33.3 %collective-permute-start = (bf16[8,32,2048]{2,1,0:T(8,128)(2,1)S(1)}, bf16[8,32,2048]{2,1,0:T(8,128)(2,1)}, u32[]{:S(2)}, u32[]{:S(2)}) collective-permute-start(bf16[8,32,2048]{2,1,0:T(8,128)(2,1)S(1)} %all-to-all-done), channel_id=1, source_target_pairs={{0,32},{32,0},{64,96},{96,64},{128,160},{160,128},{192,224},{224,1... | collective-permute-start | bytes 3145736 | tf_op jit(solution)/shard_map/ppermute | solution.py:15
  77.3 21.2 %collective-permute-start.5 = (bf16[128,2112]{0,1:T(8,128)(2,1)}, bf16[128,2112]{0,1:T(8,128)(2,1)}, u32[]{:S(2)}, u32[]{:S(2)}) collective-permute-start(bf16[128,2112]{0,1:T(8,128)(2,1)} %collective-permute-done.4), channel_id=1, source_target_pairs={{0,32},{32,64},{64,96},{96,128},{128,160},{160,192},{192,224},{224... | collective-permute-start | bytes 1622024 | tf_op jit(solution)/shard_map/ppermute | solution.py:117
  78.7 22.0 %collective-permute-start.13 = (bf16[128,2112]{0,1:T(8,128)(2,1)}, bf16[128,2112]{0,1:T(8,128)(2,1)}, u32[]{:S(2)}, u32[]{:S(2)}) collective-permute-start(bf16[128,2112]{0,1:T(8,128)(2,1)} %collective-permute-done.12), channel_id=1, source_target_pairs={{0,480},{32,0},{64,32},{96,64},{128,96},{160,128},{192,160},{224,1... | collective-permute-start | bytes 1622024 | tf_op jit(solution)/shard_map/ppermute | solution.py:119
  83.8 46.0 %copy-start.24 = (bf16[32,2048]{1,0:T(8,128)(2,1)S(1)}, bf16[32,2048]{1,0:T(8,128)(2,1)}, u32[]{:S(2)}) copy-start(bf16[32,2048]{1,0:T(8,128)(2,1)} %param.12) | copy-start | bytes 393220
  96.4 58.8 %copy-start.16 = (bf16[1,128,1408]{2,1,0:T(8,128)(2,1)S(1)}, bf16[1,128,1408]{2,1,0:T(8,128)(2,1)}, u32[]{:S(2)}) copy-start(bf16[1,128,1408]{2,1,0:T(8,128)(2,1)} %param.19) | copy-start | bytes 1081348
  98.5 14.9 %collective-permute-start.6 = (bf16[128,2112]{0,1:T(8,128)(2,1)}, bf16[128,2112]{0,1:T(8,128)(2,1)}, u32[]{:S(2)}, u32[]{:S(2)}) collective-permute-start(bf16[128,2112]{0,1:T(8,128)(2,1)} %collective-permute-done.5), channel_id=1, source_target_pairs={{0,32},{32,64},{64,96},{96,128},{128,160},{160,192},{192,224},{224... | collective-permute-start | bytes 1622024 | tf_op jit(solution)/shard_map/ppermute | solution.py:117
  102.8 19.0 %collective-permute-start.14 = (bf16[128,2112]{0,1:T(8,128)(2,1)}, bf16[128,2112]{0,1:T(8,128)(2,1)}, u32[]{:S(2)}, u32[]{:S(2)}) collective-permute-start(bf16[128,2112]{0,1:T(8,128)(2,1)} %collective-permute-done.13), channel_id=1, source_target_pairs={{0,480},{32,0},{64,32},{96,64},{128,96},{160,128},{192,160},{224,1... | collective-permute-start | bytes 1622024 | tf_op jit(solution)/shard_map/ppermute | solution.py:119
  113.5 8.4 %collective-permute-start.7 = (bf16[128,2112]{0,1:T(8,128)(2,1)}, bf16[128,2112]{0,1:T(8,128)(2,1)}, u32[]{:S(2)}, u32[]{:S(2)}) collective-permute-start(bf16[128,2112]{0,1:T(8,128)(2,1)} %collective-permute-done.6), channel_id=1, source_target_pairs={{0,32},{32,64},{64,96},{96,128},{128,160},{160,192},{192,224},{224... | collective-permute-start | bytes 1622024 | tf_op jit(solution)/shard_map/ppermute | solution.py:117
  113.8 16.0 %all-to-all-start.1 = ((bf16[16,32,128]{2,1,0:T(8,128)(2,1)}), bf16[16,32,128]{2,1,0:T(8,128)(2,1)S(1)}, u32[]{:S(2)}, u32[]{:S(2)}) async-start(bf16[16,32,128]{2,1,0:T(8,128)(2,1)} %bitcast.4), calls=%async_computation.1 | async-start | bytes 262144 | tf_op jit(solution)/shard_map/all_to_all | solution.py:91
  121.6 87.1 %all-gather.5.cloned.1.call-start = ((), (), s32[]{:S(2)}) async-start(), calls=%async_computation.5 | async-start | bytes 1179648 | tf_op jit(solution)/shard_map/all_gather | solution.py:22
  121.8 19.3 %collective-permute-start.15 = (bf16[128,2112]{0,1:T(8,128)(2,1)}, bf16[128,2112]{0,1:T(8,128)(2,1)}, u32[]{:S(2)}, u32[]{:S(2)}) collective-permute-start(bf16[128,2112]{0,1:T(8,128)(2,1)} %collective-permute-done.14), channel_id=1, source_target_pairs={{0,480},{32,0},{64,32},{96,64},{128,96},{160,128},{192,160},{224,1... | collective-permute-start | bytes 1622024 | tf_op jit(solution)/shard_map/ppermute | solution.py:119
  121.9 21.3 %collective-permute-start.8 = (bf16[128,2112]{0,1:T(8,128)(2,1)}, bf16[128,2112]{0,1:T(8,128)(2,1)}, u32[]{:S(2)}, u32[]{:S(2)}) collective-permute-start(bf16[128,2112]{0,1:T(8,128)(2,1)} %collective-permute-done.7), channel_id=1, source_target_pairs={{0,32},{32,64},{64,96},{96,128},{128,160},{160,192},{192,224},{224... | collective-permute-start | bytes 1622024 | tf_op jit(solution)/shard_map/ppermute | solution.py:117
  129.9 0.7 copy-start.19
  130.0 41.4 %copy-start.28 = (f32[32]{0:T(128)}, f32[32]{0:T(128)S(1)}, u32[]{:S(2)}) copy-start(f32[32]{0:T(128)S(1)} %add_rsqrt_fusion.1) | copy-start | bytes 388
  132.8 25.6 %copy-start.3 = (bf16[128,2112]{1,0:T(8,128)(2,1)S(1)}, bf16[128,2112]{1,0:T(8,128)(2,1)}, u32[]{:S(2)}) copy-start(bf16[128,2112]{1,0:T(8,128)(2,1)} %copy.88) | copy-start | bytes 1622020
  132.8 30.8 %copy-start.1 = (bf16[128,2112]{1,0:T(8,128)(2,1)S(1)}, bf16[128,2112]{1,0:T(8,128)(2,1)}, u32[]{:S(2)}) copy-start(bf16[128,2112]{1,0:T(8,128)(2,1)} %copy.86) | copy-start | bytes 1622020
  132.8 30.9 %copy-start.2 = (bf16[128,2112]{1,0:T(8,128)(2,1)S(1)}, bf16[128,2112]{1,0:T(8,128)(2,1)}, u32[]{:S(2)}) copy-start(bf16[128,2112]{1,0:T(8,128)(2,1)} %copy.87) | copy-start | bytes 1622020
  145.4 17.5 %copy-start.15 = (bf16[128,2112]{1,0:T(8,128)(2,1)S(1)}, bf16[128,2112]{1,0:T(8,128)(2,1)}, u32[]{:S(2)}) copy-start(bf16[128,2112]{1,0:T(8,128)(2,1)} %copy.78) | copy-start | bytes 1622020
  145.4 17.6 %copy-start.14 = (bf16[128,2112]{1,0:T(8,128)(2,1)S(1)}, bf16[128,2112]{1,0:T(8,128)(2,1)}, u32[]{:S(2)}) copy-start(bf16[128,2112]{1,0:T(8,128)(2,1)} %copy.79) | copy-start | bytes 1622020
  145.4 17.7 %copy-start.13 = (bf16[128,2112]{1,0:T(8,128)(2,1)S(1)}, bf16[128,2112]{1,0:T(8,128)(2,1)}, u32[]{:S(2)}) copy-start(bf16[128,2112]{1,0:T(8,128)(2,1)} %copy.80) | copy-start | bytes 1622020
  145.4 17.8 %copy-start.10 = (bf16[128,2112]{1,0:T(8,128)(2,1)S(1)}, bf16[128,2112]{1,0:T(8,128)(2,1)}, u32[]{:S(2)}) copy-start(bf16[128,2112]{1,0:T(8,128)(2,1)} %copy.81) | copy-start | bytes 1622020
  145.4 17.8 %copy-start.9 = (bf16[128,2112]{1,0:T(8,128)(2,1)S(1)}, bf16[128,2112]{1,0:T(8,128)(2,1)}, u32[]{:S(2)}) copy-start(bf16[128,2112]{1,0:T(8,128)(2,1)} %copy.82) | copy-start | bytes 1622020
  145.4 17.9 %copy-start.8 = (bf16[128,2112]{1,0:T(8,128)(2,1)S(1)}, bf16[128,2112]{1,0:T(8,128)(2,1)}, u32[]{:S(2)}) copy-start(bf16[128,2112]{1,0:T(8,128)(2,1)} %copy.83) | copy-start | bytes 1622020
  145.4 18.0 %copy-start.6 = (bf16[128,2112]{1,0:T(8,128)(2,1)S(1)}, bf16[128,2112]{1,0:T(8,128)(2,1)}, u32[]{:S(2)}) copy-start(bf16[128,2112]{1,0:T(8,128)(2,1)} %copy.84) | copy-start | bytes 1622020
  145.4 18.0 %copy-start.5 = (bf16[128,2112]{1,0:T(8,128)(2,1)S(1)}, bf16[128,2112]{1,0:T(8,128)(2,1)}, u32[]{:S(2)}) copy-start(bf16[128,2112]{1,0:T(8,128)(2,1)} %copy.85) | copy-start | bytes 1622020
  145.4 18.1 %copy-start.18 = (bf16[1,704,128]{1,2,0:T(8,128)(2,1)S(1)}, bf16[1,704,128]{1,2,0:T(8,128)(2,1)}, u32[]{:S(2)}) copy-start(bf16[1,704,128]{1,2,0:T(8,128)(2,1)} %copy-done.17) | copy-start | bytes 540676
  145.4 18.4 %copy-start.4 = (bf16[128,2112]{1,0:T(8,128)(2,1)S(1)}, bf16[128,2112]{1,0:T(8,128)(2,1)}, u32[]{:S(2)}) copy-start(bf16[128,2112]{1,0:T(8,128)(2,1)} %copy.89) | copy-start | bytes 1622020
  145.4 18.4 %copy-start.7 = (bf16[128,2112]{1,0:T(8,128)(2,1)S(1)}, bf16[128,2112]{1,0:T(8,128)(2,1)}, u32[]{:S(2)}) copy-start(bf16[128,2112]{1,0:T(8,128)(2,1)} %copy.90) | copy-start | bytes 1622020
  145.4 18.5 %copy-start.11 = (bf16[128,2112]{1,0:T(8,128)(2,1)S(1)}, bf16[128,2112]{1,0:T(8,128)(2,1)}, u32[]{:S(2)}) copy-start(bf16[128,2112]{1,0:T(8,128)(2,1)} %copy.91) | copy-start | bytes 1622020
  145.5 18.6 %copy-start.12 = (bf16[128,2112]{1,0:T(8,128)(2,1)S(1)}, bf16[128,2112]{1,0:T(8,128)(2,1)}, u32[]{:S(2)}) copy-start(bf16[128,2112]{1,0:T(8,128)(2,1)} %copy.92) | copy-start | bytes 1622020
  164.1 6.1 %copy-start.26 = (bf16[4096,2112]{1,0:T(8,128)(2,1)}, bf16[4096,2112]{1,0:T(8,128)(2,1)S(1)}, u32[]{:S(2)}) copy-start(bf16[4096,2112]{1,0:T(8,128)(2,1)S(1)} %constant_dynamic-update-slice_fusion) | copy-start | bytes 51904516
  208.7 16.7 %collective-permute-start.16 = (bf16[8,32,2048]{2,1,0:T(8,128)(2,1)}, bf16[8,32,2048]{2,1,0:T(8,128)(2,1)}, u32[]{:S(2)}, u32[]{:S(2)}) collective-permute-start(bf16[8,32,2048]{2,1,0:T(8,128)(2,1)} %bitcast.91), channel_id=1, source_target_pairs={{0,32},{32,0},{64,96},{96,64},{128,160},{160,128},{192,224},{224,1... | collective-permute-start | bytes 3145736 | tf_op jit(solution)/shard_map/ppermute | solution.py:15
  215.8 58.4 %all-to-all-start.2 = ((bf16[32,12,2048]{2,1,0:T(8,128)(2,1)}), bf16[32,12,2048]{2,1,0:T(8,128)(2,1)S(1)}, u32[]{:S(2)}, u32[]{:S(2)}) async-start(bf16[32,12,2048]{2,1,0:T(8,128)(2,1)} %reshape.112), calls=%async_computation.2 | async-start | bytes 4194304 | tf_op jit(solution)/shard_map/all_to_all | solution.py:126
  225.1 68.8 %all-gather.7.cloned.1.call-start = ((), (), s32[]{:S(2)}) async-start(), calls=%async_computation.6 | async-start | bytes 1622016 | tf_op jit(solution)/shard_map/all_gather | solution.py:22
  286.3 56.3 %all-to-all-start.3 = ((bf16[32,12,2048]{2,1,0:T(8,128)(2,1)}), bf16[32,12,2048]{2,1,0:T(8,128)(2,1)S(1)}, u32[]{:S(2)}, u32[]{:S(2)}) async-start(bf16[32,12,2048]{2,1,0:T(8,128)(2,1)} %reshape.114), calls=%async_computation.3 | async-start | bytes 4194304 | tf_op jit(solution)/shard_map/all_to_all | solution.py:135
  293.9 8.9 %copy-start.20 = (bf16[2816,128]{1,0:T(8,128)(2,1)S(1)}, bf16[2816,128]{1,0:T(8,128)(2,1)}, u32[]{:S(2)}) copy-start(bf16[2816,128]{1,0:T(8,128)(2,1)} %param.22) | copy-start | bytes 2162692
  295.5 6.4 %collective-permute-start.17 = (bf16[8,512,176]{1,2,0:T(8,128)(2,1)S(1)}, bf16[8,512,176]{1,2,0:T(8,128)(2,1)S(1)}, u32[]{:S(2)}, u32[]{:S(2)}) collective-permute-start(bf16[8,512,176]{1,2,0:T(8,128)(2,1)S(1)} %bitcast.89), channel_id=1, source_target_pairs={{0,32},{32,0},{64,96},{96,64},{128,160},{160,128},{192,224},{224,1... | collective-permute-start | bytes 4325384 | tf_op jit(solution)/shard_map/ppermute | solution.py:15
  342.6 15.7 %all-to-all-start.4 = ((bf16[16,32,128]{2,1,0:T(8,128)(2,1)}), bf16[16,32,128]{2,1,0:T(8,128)(2,1)}, u32[]{:S(2)}, u32[]{:S(2)}) async-start(bf16[16,32,128]{2,1,0:T(8,128)(2,1)} %bitcast.93), calls=%async_computation.4 | async-start | bytes 262144 | tf_op jit(solution)/shard_map/all_to_all | solution.py:152
Sparse Core Ops, SparseCore 0:
  173.2 35.4 all-gather.4
  229.6 37.2 all-gather.6
